TPU v7x, 256 devices: a whole 4x4x8 slice. The times are simulated.
256 devices in a mesh: island: 4 (over x_lo, core), fsdp: 64 (over x_hi, z, y).
Axes of the slice: x: 4 (x_hi: 2, x_lo: 2; x = x_hi * 2 + x_lo), y: 4, z: 8, core: 2. Of those that a mesh axis runs over, the one named last changes fastest.
Arguments:
- acts: bfloat16 [65536, 8192], P(('island', 'fsdp')), may hold values from -24 to 24
- cotangent: bfloat16 [65536, 512], P(('island', 'fsdp')), may hold values from -6 to 6
- global_params: float32 [8192, 512], P('fsdp'), may hold values from -0.12 to 0.12
- momentum: float32 [8192, 512], P('fsdp'), may hold values from -0.18 to 0.18
- island_drift: float32 [4, 8192, 512], P('island', 'fsdp'), may hold values from -0.12 to 0.12
- moment1: float32 [4, 8192, 512], P('island', 'fsdp'), may hold values from -6 to 6
- moment2: float32 [4, 8192, 512], P('island', 'fsdp'), may hold values from 0.05 to 1
Outputs:
- keys: bfloat16 [65536, 512], P(('island', 'fsdp'))
- new_global: float32 [8192, 512], P('fsdp')
- new_momentum: float32 [8192, 512], P('fsdp')
- moment1_out: float32 [4, 8192, 512], P('island', 'fsdp')
- moment2_out: float32 [4, 8192, 512], P('island', 'fsdp')
All inputs are finite; a program needn't handle non-finite values.
Results may differ from a plain program's by a relative error of at most 0.0049.
Values may be sent and summed in bfloat16 or wider, within the bound.
No kernel may reach another device: no remote copies, remote signals or barrier semaphores. Data moves between devices by JAX's collectives and lax.ppermute only.
A program may use at most 128 MiB of HBM per device.

v0:
```python
import jax
import jax.numpy as jnp
from jax import lax
from jax.sharding import PartitionSpec as P

D = 8192
beta_one = 0.9
beta_two = 0.95
epsilon = 1e-08
inner_rate = 0.05
decay_rate = 0.1
outer_rate = 0.7
nesterov = 0.9


def per_device(acts, cotangent, global_params, momentum, island_drift, moment1, moment2):
    fsdp_count = lax.axis_size("fsdp")
    island_count = lax.axis_size("island")
    scale = (acts.shape[0] * fsdp_count) ** (-0.5)
    grad = lax.psum_scatter(
        lax.dot_general(
            acts, cotangent, (((0,), (0,)), ((), ())), preferred_element_type=jnp.float32
        ),
        "fsdp",
        scatter_dimension=0,
        tiled=True,
    )
    grad = grad * scale
    drift = island_drift[0]
    first = beta_one * moment1[0] + (1.0 - beta_one) * grad
    second = beta_two * moment2[0] + (1.0 - beta_two) * grad * grad
    step = first / (jnp.sqrt(second) + epsilon) + decay_rate * (global_params - drift)
    pseudo = drift + inner_rate * step
    mean = lax.psum(pseudo, "island") / island_count
    new_momentum = nesterov * momentum + mean
    new_global = global_params - outer_rate * (mean + nesterov * new_momentum)
    weights = new_global.astype(jnp.bfloat16)
    keys = jnp.dot(
        acts,
        lax.all_gather(weights, "fsdp", axis=0, tiled=True),
        preferred_element_type=jnp.float32,
    )
    keys = (keys * D ** (-0.5)).astype(jnp.bfloat16)
    return (keys, new_global, new_momentum, first[None], second[None])


def solution(mesh):
    return jax.shard_map(
        per_device,
        mesh=mesh,
        in_specs=(
            P(("island", "fsdp"), None),
            P(("island", "fsdp"), None),
            P("fsdp", None),
            P("fsdp", None),
            P("island", "fsdp", None),
            P("island", "fsdp", None),
            P("island", "fsdp", None),
        ),
        out_specs=(
            P(("island", "fsdp"), None),
            P("fsdp", None),
            P("fsdp", None),
            P("island", "fsdp", None),
            P("island", "fsdp", None),
        ),
        check_vma=False,
    )
```

profile of v0, /device:TPU:8, one launch (start us, length us, event | category | flops | bytes accessed | tf_op | source)
XLA Modules:
  0.0 632.4 jit_solution(935737495468121115)
XLA Ops:
  7.2 0.0 copy-start
  7.2 0.0 reduce-scatter.2.cloned.1.call-start
  7.2 0.9 copy-done
  8.1 10.3 %fusion.8 = f32[8192,512]{1,0:T(8,128)} fusion(bf16[256,8192]{1,0:T(8,128)(2,1)} %param.7, bf16[256,512]{1,0:T(8,128)(2,1)S(1)} %copy-done), kind=kOutput, calls=%fused_computation.15 | convolution fusion | flops 2147483648 | bytes 21233664 | tf_op jit(solution)/shard_map/dot_general | solution.py:21
  18.4 0.0 copy-start.1
  18.4 0.0 copy-start.3
  18.4 0.0 copy-start.4
  18.4 0.0 copy-start.5
  18.4 0.0 copy-start.2
  18.5 0.0 reduce-scatter.2.cloned.1.call-update
  18.5 0.0 all-reduce.2.cloned.1.call-start
  18.5 400.2 %reduce-scatter.2.cloned.1.call-done = f32[128,512]{1,0:T(8,128)} async-done(((f32[8192,512]{1,0:T(8,128)}), f32[128,512]{1,0:T(8,128)}) %reduce-scatter.2.cloned.1.call-update) | async-done | bytes 262160 | tf_op jit(solution)/shard_map/reduce_scatter | solution.py:20
  418.8 0.0 copy-done.1
  418.8 0.0 copy-done.3
  418.8 0.0 copy-done.4
  418.8 0.0 copy-done.5
  418.8 2.0 fusion.6
  420.8 0.0 all-reduce.2.cloned.1.call-update
  420.8 0.0 all-gather.2.cloned.1.call-start
  420.9 42.0 %all-reduce.2.cloned.1.call-done = f32[128,512]{1,0:T(8,128)} async-done(((f32[128,512]{1,0:T(8,128)}), f32[128,512]{1,0:T(8,128)}) %all-reduce.2.cloned.1.call-update) | async-done | bytes 262160 | tf_op jit(solution)/shard_map/psum | solution.py:34
  462.9 0.0 copy-done.2
  462.9 1.9 fusion.7
  464.8 0.0 all-gather.2.cloned.1.call-update
  464.8 153.3 %all-gather.2.cloned.1.call-done = bf16[8192,512]{1,0:T(8,128)(2,1)} async-done(((bf16[128,512]{1,0:T(8,128)(2,1)}), bf16[8192,512]{1,0:T(8,128)(2,1)}) %all-gather.2.cloned.1.call-update) | async-done | bytes 8388624 | tf_op jit(solution)/shard_map/all_gather | solution.py:40
  618.1 6.9 %fusion.1 = bf16[256,512]{0,1:T(8,128)(2,1)S(1)} fusion(bf16[8192,512]{1,0:T(8,128)(2,1)} %all-gather.2.cloned.1.call-done, bf16[256,8192]{1,0:T(8,128)(2,1)} %param.7), kind=kOutput, calls=%fused_computation.2 | convolution fusion | flops 2147745792 | bytes 12845056 | tf_op jit(solution)/shard_map/dot_general | solution.py:38
  625.1 0.8 copy.12
Async XLA Ops:
  7.2 1.0 copy-start
  7.2 411.6 %reduce-scatter.2.cloned.1.call-start = ((), (), s32[]{:S(2)}) async-start(), calls=%async_computation.1 | async-start | bytes 17039360 | tf_op jit(solution)/shard_map/reduce_scatter | solution.py:20
  18.4 400.3 %copy-start.1 = (f32[128,512]{1,0:T(8,128)S(1)}, f32[128,512]{1,0:T(8,128)}, u32[]{:S(2)}) copy-start(f32[128,512]{1,0:T(8,128)} %param.9) | copy-start | bytes 786436
  18.4 400.3 %copy-start.3 = (f32[1,128,512]{2,1,0:T(8,128)S(1)}, f32[1,128,512]{2,1,0:T(8,128)}, u32[]{:S(2)}) copy-start(f32[1,128,512]{2,1,0:T(8,128)} %param.13) | copy-start | bytes 786436
  18.4 400.3 %copy-start.4 = (f32[1,128,512]{2,1,0:T(8,128)S(1)}, f32[1,128,512]{2,1,0:T(8,128)}, u32[]{:S(2)}) copy-start(f32[1,128,512]{2,1,0:T(8,128)} %param.12) | copy-start | bytes 786436
  18.4 400.3 %copy-start.5 = (f32[1,128,512]{2,1,0:T(8,128)S(1)}, f32[1,128,512]{2,1,0:T(8,128)}, u32[]{:S(2)}) copy-start(f32[1,128,512]{2,1,0:T(8,128)} %param.11) | copy-start | bytes 786436
  18.4 444.5 %copy-start.2 = (f32[128,512]{1,0:T(8,128)S(1)}, f32[128,512]{1,0:T(8,128)}, u32[]{:S(2)}) copy-start(f32[128,512]{1,0:T(8,128)} %param.10) | copy-start | bytes 786436
  18.5 444.4 %all-reduce.2.cloned.1.call-start = ((), (), s32[]{:S(2)}) async-start(), calls=%async_computation.2 | async-start | bytes 524288 | tf_op jit(solution)/shard_map/psum | solution.py:34
  420.8 197.3 %all-gather.2.cloned.1.call-start = ((), (), s32[]{:S(2)}) async-start(), calls=%async_computation.3 | async-start | bytes 8519680 | tf_op jit(solution)/shard_map/all_gather | solution.py:40
Sparse Core Ops, SparseCore 0:
  18.6 400.1 reduce-scatter.1
  422.0 40.9 all-reduce.1
  467.1 150.9 all-gather.1
where the time goes:
time: 633 us; the launch traced here: 632 us
  waiting for transfers between devices  596 us (94%)
  matrix products  17.3 us (3%)
  between operations  13.8 us (2%)
    reduce_scatter x1, waiting for transfers between devices, per_device(): lax.psum_scatter(lax.dot_general(acts, cotangent, (((0,), (0,)), ((), ())...  400 us
    all_gather x1, waiting for transfers between devices, per_device(): lax.all_gather(weights, 'fsdp', axis=0, tiled=True)  153 us
    psum x1, waiting for transfers between devices, per_device(): mean = lax.psum(pseudo, 'island') / island_count  42 us
  transfers between devices with their start and end apart: 3, of which 3 were waited for; matrix products, arithmetic and copies ran while one was open for 0% of the time, Pallas kernels for 0%

commit v1 on v0

--- a/solution.py
+++ b/solution.py
@@ -31,7 +31,7 @@
     second = beta_two * moment2[0] + (1.0 - beta_two) * grad * grad
     step = first / (jnp.sqrt(second) + epsilon) + decay_rate * (global_params - drift)
     pseudo = drift + inner_rate * step
-    mean = lax.psum(pseudo, "island") / island_count
+    mean = jnp.sum(lax.all_gather(pseudo, "island"), axis=0) / island_count
     new_momentum = nesterov * momentum + mean
     new_global = global_params - outer_rate * (mean + nesterov * new_momentum)
     weights = new_global.astype(jnp.bfloat16)

time: 633 us -> 614 us (0.970)
  waiting for transfers between devices: 596 us -> 576 us
    psum x1 -> x0, waiting for transfers between devices: 42 us -> none  [per_device(): mean = lax.psum(pseudo, 'island') / island_count]
    all_gather x0 -> x1, waiting for transfers between devices: none -> 22.7 us  [per_device(): mean = jnp.sum(lax.all_gather(pseudo, 'island'), axis=0) / island_count]
where the time goes in v1:
time: 614 us; the launch traced here: 613 us
  waiting for transfers between devices  576 us (94%)
  matrix products  17.3 us (3%)
  between operations  13.8 us (2%)
    reduce_scatter x1, waiting for transfers between devices, per_device(): lax.psum_scatter(lax.dot_general(acts, cotangent, (((0,), (0,)), ((), ())...  400 us
    all_gather x1, waiting for transfers between devices, per_device(): lax.all_gather(weights, 'fsdp', axis=0, tiled=True)  153 us
    all_gather x1, waiting for transfers between devices, per_device(): mean = jnp.sum(lax.all_gather(pseudo, 'island'), axis=0) / island_count  22.7 us
  transfers between devices with their start and end apart: 3, of which 3 were waited for; matrix products, arithmetic and copies ran while one was open for 0% of the time, Pallas kernels for 0%

profile of v1, /device:TPU:8, one launch (start us, length us, event | category | flops | bytes accessed | tf_op | source)
XLA Modules:
  0.0 613.4 jit_solution(15586686653360926640)
XLA Ops:
  7.2 0.0 copy-start
  7.2 0.0 reduce-scatter.2.cloned.1.call-start
  7.2 0.9 copy-done
  8.1 10.3 %fusion.8 = f32[8192,512]{1,0:T(8,128)} fusion(bf16[256,8192]{1,0:T(8,128)(2,1)} %param.7, bf16[256,512]{1,0:T(8,128)(2,1)S(1)} %copy-done), kind=kOutput, calls=%fused_computation.15 | convolution fusion | flops 2147483648 | bytes 21233664 | tf_op jit(solution)/shard_map/dot_general | solution.py:21
  18.4 0.0 copy-start.1
  18.4 0.0 copy-start.3
  18.4 0.0 copy-start.4
  18.4 0.0 copy-start.5
  18.4 0.0 copy-start.2
  18.5 0.0 reduce-scatter.2.cloned.1.call-update
  18.5 0.0 all-gather.6.cloned.1.call-start
  18.5 400.2 %reduce-scatter.2.cloned.1.call-done = f32[128,512]{1,0:T(8,128)} async-done(((f32[8192,512]{1,0:T(8,128)}), f32[128,512]{1,0:T(8,128)}) %reduce-scatter.2.cloned.1.call-update) | async-done | bytes 262160 | tf_op jit(solution)/shard_map/reduce_scatter | solution.py:20
  418.8 0.0 copy-done.1
  418.8 0.0 copy-done.3
  418.8 0.0 copy-done.4
  418.8 0.0 copy-done.5
  418.8 2.0 fusion.6
  420.8 0.0 all-gather.6.cloned.1.call-update
  420.8 0.0 all-gather.4.cloned.1.call-start
  420.9 22.7 %all-gather.6.cloned.1.call-done = f32[512,512]{1,0:T(8,128)} async-done(((f32[128,512]{1,0:T(8,128)}), f32[512,512]{1,0:T(8,128)}) %all-gather.6.cloned.1.call-update) | async-done | bytes 1048592 | tf_op jit(solution)/shard_map/all_gather | solution.py:34
  443.6 1.3 reduce_sum.9
  444.9 0.0 copy-done.2
  444.9 0.9 fusion.7
  445.8 0.0 all-gather.4.cloned.1.call-update
  445.9 153.2 %all-gather.4.cloned.1.call-done = bf16[8192,512]{1,0:T(8,128)(2,1)} async-done(((bf16[128,512]{1,0:T(8,128)(2,1)}), bf16[8192,512]{1,0:T(8,128)(2,1)}) %all-gather.4.cloned.1.call-update) | async-done | bytes 8388624 | tf_op jit(solution)/shard_map/all_gather | solution.py:40
  599.1 6.9 %fusion.1 = bf16[256,512]{0,1:T(8,128)(2,1)S(1)} fusion(bf16[8192,512]{1,0:T(8,128)(2,1)} %all-gather.4.cloned.1.call-done, bf16[256,8192]{1,0:T(8,128)(2,1)} %param.7), kind=kOutput, calls=%fused_computation.2 | convolution fusion | flops 2147745792 | bytes 12845056 | tf_op jit(solution)/shard_map/dot_general | solution.py:38
  606.0 0.8 copy.12
Async XLA Ops:
  7.2 1.0 copy-start
  7.2 411.6 %reduce-scatter.2.cloned.1.call-start = ((), (), s32[]{:S(2)}) async-start(), calls=%async_computation.1 | async-start | bytes 17039360 | tf_op jit(solution)/shard_map/reduce_scatter | solution.py:20
  18.4 400.3 %copy-start.1 = (f32[128,512]{1,0:T(8,128)S(1)}, f32[128,512]{1,0:T(8,128)}, u32[]{:S(2)}) copy-start(f32[128,512]{1,0:T(8,128)} %param.9) | copy-start | bytes 786436
  18.4 400.3 %copy-start.3 = (f32[1,128,512]{2,1,0:T(8,128)S(1)}, f32[1,128,512]{2,1,0:T(8,128)}, u32[]{:S(2)}) copy-start(f32[1,128,512]{2,1,0:T(8,128)} %param.13) | copy-start | bytes 786436
  18.4 400.3 %copy-start.4 = (f32[1,128,512]{2,1,0:T(8,128)S(1)}, f32[1,128,512]{2,1,0:T(8,128)}, u32[]{:S(2)}) copy-start(f32[1,128,512]{2,1,0:T(8,128)} %param.12) | copy-start | bytes 786436
  18.4 400.3 %copy-start.5 = (f32[1,128,512]{2,1,0:T(8,128)S(1)}, f32[1,128,512]{2,1,0:T(8,128)}, u32[]{:S(2)}) copy-start(f32[1,128,512]{2,1,0:T(8,128)} %param.11) | copy-start | bytes 786436
  18.4 426.5 %copy-start.2 = (f32[128,512]{1,0:T(8,128)S(1)}, f32[128,512]{1,0:T(8,128)}, u32[]{:S(2)}) copy-start(f32[128,512]{1,0:T(8,128)} %param.10) | copy-start | bytes 786436
  18.5 425.1 %all-gather.6.cloned.1.call-start = ((), (), s32[]{:S(2)}) async-start(), calls=%async_computation.3 | async-start | bytes 1310720 | tf_op jit(solution)/shard_map/all_gather | solution.py:34
  420.8 178.2 %all-gather.4.cloned.1.call-start = ((), (), s32[]{:S(2)}) async-start(), calls=%async_computation.2 | async-start | bytes 8519680 | tf_op jit(solution)/shard_map/all_gather | solution.py:40
Sparse Core Ops, SparseCore 0:
  18.6 400.1 reduce-scatter.1
  421.2 22.3 all-gather.5
  447.8 151.2 all-gather.3

commit v2 on v0

--- a/solution.py
+++ b/solution.py
@@ -37,7 +37,9 @@
     weights = new_global.astype(jnp.bfloat16)
     keys = jnp.dot(
         acts,
-        lax.all_gather(weights, "fsdp", axis=0, tiled=True),
+        jnp.concatenate(
+            lax.all_to_all(jnp.stack([weights] * lax.axis_size("fsdp")), "fsdp", 0, 0), axis=0
+        ),
         preferred_element_type=jnp.float32,
     )
     keys = (keys * D ** (-0.5)).astype(jnp.bfloat16)

time: 633 us -> 677 us (1.070)
  blocking collectives: 0 us -> 199 us
  waiting for transfers between devices: 596 us -> 442 us
    all_to_all x0 -> x1, blocking collectives: none -> 199 us  [per_device(): lax.all_to_all(jnp.stack([weights] * lax.axis_size('fsdp')), 'fsdp', 0, 0)]
    all_gather x1 -> x0, waiting for transfers between devices: 153 us -> none  [per_device(): lax.all_gather(weights, 'fsdp', axis=0, tiled=True)]
  transfers between devices with their start and end apart: 3 -> 2, of which waited for: 3 -> 2; matrix products, arithmetic and copies ran while one was open for 0% -> 0% of each run, Pallas kernels for 0% -> 0%
where the time goes in v2:
time: 677 us; the launch traced here: 675 us
  waiting for transfers between devices  442 us (65%)
  blocking collectives  199 us (29%)
  between operations  14.1 us (2%)
  matrix products  12.7 us (2%)
    reduce_scatter x1, waiting for transfers between devices, per_device(): lax.psum_scatter(lax.dot_general(acts, cotangent, (((0,), (0,)), ((), ())...  400 us
    all_to_all x1, blocking collectives, per_device(): lax.all_to_all(jnp.stack([weights] * lax.axis_size('fsdp')), 'fsdp', 0, 0)  199 us
    psum x1, waiting for transfers between devices, per_device(): mean = lax.psum(pseudo, 'island') / island_count  42.1 us
  transfers between devices with their start and end apart: 2, of which 2 were waited for; matrix products, arithmetic and copies ran while one was open for 0% of the time, Pallas kernels for 0%

profile of v2, /device:TPU:8, one launch (start us, length us, event | category | flops | bytes accessed | tf_op | source)
XLA Modules:
  0.0 675.1 jit_solution(361592737976531181)
XLA Ops:
  7.2 0.0 copy-start
  7.2 0.0 reduce-scatter.2.cloned.1.call-start
  7.2 0.9 copy-done
  8.1 10.3 %fusion.8 = f32[8192,512]{1,0:T(8,128)} fusion(bf16[256,8192]{1,0:T(8,128)(2,1)} %param.7, bf16[256,512]{1,0:T(8,128)(2,1)S(1)} %copy-done), kind=kOutput, calls=%fused_computation.15 | convolution fusion | flops 2147483648 | bytes 21233664 | tf_op jit(solution)/shard_map/dot_general | solution.py:21
  18.4 0.0 copy-start.2
  18.4 0.0 copy-start.4
  18.4 0.0 copy-start.5
  18.4 0.0 copy-start.6
  18.4 0.0 copy-start.3
  18.4 0.0 reduce-scatter.2.cloned.1.call-update
  18.5 0.0 all-reduce.2.cloned.1.call-start
  18.5 400.2 %reduce-scatter.2.cloned.1.call-done = f32[128,512]{1,0:T(8,128)} async-done(((f32[8192,512]{1,0:T(8,128)}), f32[128,512]{1,0:T(8,128)}) %reduce-scatter.2.cloned.1.call-update) | async-done | bytes 262160 | tf_op jit(solution)/shard_map/reduce_scatter | solution.py:20
  418.8 0.0 copy-done.2
  418.8 0.0 copy-done.4
  418.8 0.0 copy-done.5
  418.8 0.0 copy-done.6
  418.8 2.0 fusion.6
  420.8 0.0 all-reduce.2.cloned.1.call-update
  420.8 42.1 %all-reduce.2.cloned.1.call-done = f32[128,512]{1,0:T(8,128)} async-done(((f32[128,512]{1,0:T(8,128)}), f32[128,512]{1,0:T(8,128)}) %all-reduce.2.cloned.1.call-update) | async-done | bytes 262160 | tf_op jit(solution)/shard_map/psum | solution.py:34
  462.9 0.0 copy-done.3
  462.9 1.8 fusion.7
  464.7 1.0 stack.2
  465.8 0.0 copy-start.1
  465.8 199.2 %all_to_all.5 = bf16[64,128,512]{2,1,0:T(8,128)(2,1)S(1)} all-to-all(bf16[64,128,512]{2,1,0:T(8,128)(2,1)S(1)} %stack.2), channel_id=1, replica_groups=mesh['island'=4,'fsdp'=64] {'fsdp'}, dimensions={0} | all-to-all | bytes 16777216 | tf_op jit(solution)/shard_map/all_to_all | solution.py:41
  665.0 0.0 copy-done.1
  665.0 2.4 fusion.1
  667.4 0.8 copy.12
Async XLA Ops:
  7.2 1.0 copy-start
  7.2 411.6 %reduce-scatter.2.cloned.1.call-start = ((), (), s32[]{:S(2)}) async-start(), calls=%async_computation.2 | async-start | bytes 17039360 | tf_op jit(solution)/shard_map/reduce_scatter | solution.py:20
  18.4 400.3 %copy-start.2 = (f32[128,512]{1,0:T(8,128)S(1)}, f32[128,512]{1,0:T(8,128)}, u32[]{:S(2)}) copy-start(f32[128,512]{1,0:T(8,128)} %param.9) | copy-start | bytes 786436
  18.4 400.3 %copy-start.4 = (f32[1,128,512]{2,1,0:T(8,128)S(1)}, f32[1,128,512]{2,1,0:T(8,128)}, u32[]{:S(2)}) copy-start(f32[1,128,512]{2,1,0:T(8,128)} %param.13) | copy-start | bytes 786436
  18.4 400.3 %copy-start.5 = (f32[1,128,512]{2,1,0:T(8,128)S(1)}, f32[1,128,512]{2,1,0:T(8,128)}, u32[]{:S(2)}) copy-start(f32[1,128,512]{2,1,0:T(8,128)} %param.12) | copy-start | bytes 786436
  18.4 400.3 %copy-start.6 = (f32[1,128,512]{2,1,0:T(8,128)S(1)}, f32[1,128,512]{2,1,0:T(8,128)}, u32[]{:S(2)}) copy-start(f32[1,128,512]{2,1,0:T(8,128)} %param.11) | copy-start | bytes 786436
  18.4 444.5 %copy-start.3 = (f32[128,512]{1,0:T(8,128)S(1)}, f32[128,512]{1,0:T(8,128)}, u32[]{:S(2)}) copy-start(f32[128,512]{1,0:T(8,128)} %param.10) | copy-start | bytes 786436
  18.5 444.4 %all-reduce.2.cloned.1.call-start = ((), (), s32[]{:S(2)}) async-start(), calls=%async_computation.3 | async-start | bytes 524288 | tf_op jit(solution)/shard_map/psum | solution.py:34
  465.8 199.3 %copy-start.1 = (bf16[256,8192]{1,0:T(8,128)(2,1)S(1)}, bf16[256,8192]{1,0:T(8,128)(2,1)}, u32[]{:S(2)}) copy-start(bf16[256,8192]{1,0:T(8,128)(2,1)} %param.7) | copy-start | bytes 12582916
Sparse Core Ops, SparseCore 0:
  18.6 400.1 reduce-scatter.1
  422.0 40.9 all-reduce.1
